TPU v7x, 32 devices: a whole 2x2x4 slice. The times are simulated.
32 devices in a mesh: dp: 4 (over x, core), fsdp: 8 (over z, y).
Axes of the slice: x: 2, y: 2, z: 4, core: 2. Of those that a mesh axis runs over, the one named last changes fastest.
Arguments:
- tokens: bfloat16 [8192, 640], P(('dp', 'fsdp')), may hold values from -6 to 6
- cotangent: bfloat16 [8192, 640], P(('dp', 'fsdp')), may hold values from -6 to 6
- masked_pos: int32 [8192], P(('dp', 'fsdp')), may hold values from 0 to 1
- labels: int32 [8192], P(('dp', 'fsdp')), may hold values from 0 to 3
- decoder: bfloat16 [4, 640], replicated, may hold values from -0.375 to 0.375
- master: float32 [640, 12800], P('fsdp'), may hold values from -0.6324555 to 0.6324555
- small_params: float32 [640, 16], P('fsdp'), may hold values from -0.8 to 1.4
- small_first: float32 [640, 16], P('fsdp'), may hold values from -128 to 128
- small_second: float32 [640, 16], P('fsdp'), may hold values from 163.84 to 4096
- block_slots: int32 [40], replicated, may hold values from 0 to 39, as said below
- first_moment: float32 [40, 640, 320], P('fsdp'), may hold values from -128 to 128
- second_moment: float32 [40, 640, 320], P('fsdp'), may hold values from 163.84 to 4096
- left_bases: float32 [40, 640, 640], P('fsdp'), may hold values from -1 to 1, as said below
- right_bases: float32 [40, 320, 320], P('fsdp'), may hold values from -1 to 1, as said below
Outputs:
- out_tokens: bfloat16 [8192, 640], P(('dp', 'fsdp'))
- grad_tokens: bfloat16 [8192, 640], P(('dp', 'fsdp'))
- grad_weights: float32 [640, 12800], P('fsdp')
- grad_small: float32 [640, 16], P('fsdp')
- new_first: float32 [40, 640, 320], P('fsdp')
- new_second: float32 [40, 640, 320], P('fsdp')
- new_master: float32 [640, 12800], P('fsdp')
- new_copy: bfloat16 [640, 12800], P('fsdp')
- new_small: float32 [640, 16], P('fsdp')
- new_small_first: float32 [640, 16], P('fsdp')
- new_small_second: float32 [640, 16], P('fsdp')
- loss_accuracy: float32 [5], replicated
- counts: int32 [4], replicated
Inputs may be any that keep to these rules, and one draw needn't show every extreme that they name: Distinct slot numbers; block b (columns b * 320 to (b + 1) * 320 - 1 of the weights) keeps its optimizer state in slot block_slots[b], held by fsdp index block_slots[b] // 5; at most 5 blocks on one index. `left_bases`: each slot's matrix is orthogonal. `right_bases`: each slot's matrix is orthogonal.
All inputs are finite; a program needn't handle non-finite values.
Results may differ from a plain program's by a relative error of at most 0.013.
The roundings to bfloat16 on the way count: a program that leaves them out, or rounds other values in their place, can miss the bound.
Values may be sent and summed in bfloat16 or wider, within the bound.
No kernel may reach another device: no remote copies, remote signals or barrier semaphores. Data moves between devices by JAX's collectives and lax.ppermute only.
A program may use at most 256 MiB of HBM per device.

v0:
```python
import jax
import jax.numpy as jnp
from jax import lax
from jax.sharding import PartitionSpec as P

HEAD_DIM = 32
SEQ_LEN = 256
STEP = 5
EPS_NORM = 1e-05
EPS_ADAM = 1e-08
BETA_FIRST = 0.5
BETA_SECOND = 0.5
RATE_MATRIX = 0.02
RATE_VECTOR = 0.05
EXACT_PRECISION = lax.Precision.HIGHEST


def normalize_layer(rows_in, norm_gain, norm_shift):
    centred = rows_in - jnp.mean(rows_in, axis=-1, keepdims=True)
    variance = jnp.mean(centred * centred, axis=-1, keepdims=True)
    return centred * lax.rsqrt(variance + EPS_NORM) * norm_gain + norm_shift


def exact_gelu(inputs):
    return jax.nn.gelu(inputs, approximate=False)


def adam_direction(first_new, second_new):
    return (
        first_new
        / (1.0 - BETA_FIRST**STEP)
        / (jnp.sqrt(second_new / (1.0 - BETA_SECOND**STEP)) + EPS_ADAM)
    )


def contract_rows(left_mat, right_mat):
    return lax.dot_general(
        left_mat, right_mat, (((0,), (0,)), ((), ())), preferred_element_type=jnp.float32
    )


def times_transpose(left_mat, right_mat):
    return lax.dot_general(
        left_mat, right_mat, (((1,), (1,)), ((), ())), preferred_element_type=jnp.float32
    )


def block_scores(queries, key_rows):
    return jnp.einsum(
        "slhd,smhd->shlm", queries, key_rows, preferred_element_type=jnp.float32
    ) * HEAD_DIM ** (-0.5)


def attend_block(weight_blocks):
    queries, key_rows, values = weight_blocks
    scores = block_scores(queries, key_rows)
    highest = jnp.max(scores, axis=-1, keepdims=True)
    exponent = jnp.exp(scores - highest)
    totals = jnp.sum(exponent, axis=-1, keepdims=True)
    weights_soft = (exponent / totals).astype(jnp.bfloat16)
    mixed_rows = jnp.einsum(
        "shlm,smhd->slhd", weights_soft, values, preferred_element_type=jnp.float32
    )
    return (mixed_rows.astype(jnp.bfloat16), (highest + jnp.log(totals))[..., 0])


def attend_back(weight_blocks):
    queries, key_rows, values, log_total, d_attended = weight_blocks
    probabilities = jnp.exp(block_scores(queries, key_rows) - log_total[..., None])
    d_values = jnp.einsum(
        "shlm,slhd->smhd",
        probabilities.astype(jnp.bfloat16),
        d_attended,
        preferred_element_type=jnp.float32,
    )
    d_probs = jnp.einsum("slhd,smhd->shlm", d_attended, values, preferred_element_type=jnp.float32)
    d_scores = (
        probabilities * (d_probs - jnp.sum(probabilities * d_probs, axis=-1, keepdims=True))
    ).astype(jnp.bfloat16)
    d_queries = jnp.einsum(
        "shlm,smhd->slhd", d_scores, key_rows, preferred_element_type=jnp.float32
    ) * HEAD_DIM ** (-0.5)
    d_keys = jnp.einsum(
        "shlm,slhd->smhd", d_scores, queries, preferred_element_type=jnp.float32
    ) * HEAD_DIM ** (-0.5)
    return (
        d_queries.astype(jnp.bfloat16),
        d_keys.astype(jnp.bfloat16),
        d_values.astype(jnp.bfloat16),
    )


def local(
    tokens,
    cotangent,
    masked_pos,
    labels,
    decoder,
    master,
    small_params,
    small_first,
    small_second,
    block_slots,
    first_moment,
    second_moment,
    left_bases,
    right_bases,
):
    model_width = decoder.shape[1]
    hidden = (master.shape[1] - 4 * model_width) // 2
    heads_count = model_width // HEAD_DIM
    token_count = tokens.shape[0]
    local_weights = master.astype(jnp.bfloat16)
    local_small = small_params.astype(jnp.bfloat16)
    weights, small_all = (
        lax.all_gather(local_weights, "fsdp", axis=0, tiled=True),
        lax.all_gather(local_small, "fsdp", axis=0, tiled=True),
    )
    params = small_all.astype(jnp.float32)
    gain_one, shift_one, bias_query, bias_value, bias_output, gain_two, shift_two, bias_down = [
        params[:, column] for column in range(8)
    ]
    bias_up = params[:, 8:].reshape(hidden)
    rows_in = tokens.astype(jnp.float32)
    normed = normalize_layer(rows_in, gain_one, shift_one).astype(jnp.bfloat16)
    bias_qkv = jnp.concatenate([bias_query, jnp.zeros_like(bias_query), bias_value])
    projected = (
        jnp.dot(normed, weights[:, : 3 * model_width], preferred_element_type=jnp.float32)
        + bias_qkv
    ).astype(jnp.bfloat16)
    seq_count = token_count // SEQ_LEN
    per_block = max(1, min(seq_count, 512 // SEQ_LEN))
    block_shape = (seq_count // per_block, per_block, SEQ_LEN, heads_count, HEAD_DIM)
    queries = projected[:, :model_width].reshape(block_shape)
    key_rows = projected[:, model_width : 2 * model_width].reshape(block_shape)
    values = projected[:, 2 * model_width :].reshape(block_shape)
    attention_result, log_total = lax.map(attend_block, (queries, key_rows, values))
    attention_result = attention_result.reshape(token_count, model_width)
    middle = (
        rows_in
        + jnp.dot(
            attention_result,
            weights[:, 3 * model_width : 4 * model_width],
            preferred_element_type=jnp.float32,
        )
        + bias_output
    )
    normed_two = normalize_layer(middle, gain_two, shift_two).astype(jnp.bfloat16)
    pre_active = (
        jnp.dot(
            normed_two,
            weights[:, 4 * model_width : 4 * model_width + hidden],
            preferred_element_type=jnp.float32,
        )
        + bias_up
    )
    active = exact_gelu(pre_active).astype(jnp.bfloat16)
    output_rows = (
        middle + times_transpose(active, weights[:, 4 * model_width + hidden :]) + bias_down
    )
    out_tokens = output_rows.astype(jnp.bfloat16)
    logits = times_transpose(out_tokens, decoder)
    log_norm = jax.nn.logsumexp(logits, axis=-1)
    one_hot = (labels[:, None] == jnp.arange(decoder.shape[0], dtype=jnp.int32)[None, :]).astype(
        jnp.float32
    )
    hidden_tokens = masked_pos.astype(jnp.float32)
    chosen = one_hot * hidden_tokens[:, None]
    entropy = log_norm - jnp.sum(one_hot * logits, axis=-1)
    right_prob = jnp.sum(one_hot * jnp.exp(logits - log_norm[:, None]), axis=-1)
    local_sums = jnp.concatenate(
        [jnp.sum(hidden_tokens * entropy)[None], jnp.sum(chosen * right_prob[:, None], axis=0)]
    )
    global_sums, global_counts = lax.psum((local_sums, jnp.sum(chosen, axis=0)), ("dp", "fsdp"))
    loss_accuracy = jnp.concatenate(
        [
            global_sums[:1] / jnp.maximum(jnp.sum(global_counts), 1.0),
            global_sums[1:] / jnp.maximum(global_counts, 1.0),
        ]
    )
    counts = global_counts.astype(jnp.int32)
    weights_back, small_back = (
        lax.all_gather(local_weights, "fsdp", axis=0, tiled=True),
        lax.all_gather(local_small, "fsdp", axis=0, tiled=True),
    )
    params_back = small_back.astype(jnp.float32)
    back_rows = cotangent.astype(jnp.float32)
    d_active = jnp.dot(
        cotangent, weights_back[:, 4 * model_width + hidden :], preferred_element_type=jnp.float32
    )
    unused, gelu_pull = jax.vjp(exact_gelu, pre_active)
    d_pre = gelu_pull(d_active)[0].astype(jnp.bfloat16)
    d_normed_two = times_transpose(
        d_pre, weights_back[:, 4 * model_width : 4 * model_width + hidden]
    )
    unused, norm_pull_two = jax.vjp(normalize_layer, middle, params_back[:, 5], params_back[:, 6])
    d_middle_norm, d_gain_two, d_shift_two = norm_pull_two(d_normed_two)
    d_middle = back_rows + d_middle_norm
    d_branch = d_middle.astype(jnp.bfloat16)
    d_attended = times_transpose(
        d_branch, weights_back[:, 3 * model_width : 4 * model_width]
    ).astype(jnp.bfloat16)
    d_queries, d_keys, d_values = lax.map(
        attend_back, (queries, key_rows, values, log_total, d_attended.reshape(block_shape))
    )
    d_projected = jnp.concatenate(
        [
            d_queries.reshape(token_count, model_width),
            d_keys.reshape(token_count, model_width),
            d_values.reshape(token_count, model_width),
        ],
        axis=1,
    )
    d_normed = times_transpose(d_projected, weights_back[:, : 3 * model_width])
    unused, norm_pull_one = jax.vjp(normalize_layer, rows_in, params_back[:, 0], params_back[:, 1])
    d_rows_norm, d_gain_one, d_shift_one = norm_pull_one(d_normed)
    grad_tokens = (d_middle + d_rows_norm).astype(jnp.bfloat16)
    grad_w_local = jnp.concatenate(
        [
            contract_rows(normed, d_projected),
            contract_rows(attention_result, d_branch),
            contract_rows(normed_two, d_pre),
            contract_rows(cotangent, active),
        ],
        axis=1,
    )
    proj_sums = jnp.sum(d_projected.astype(jnp.float32), axis=0)
    small_cols = jnp.stack(
        [
            d_gain_one,
            d_shift_one,
            proj_sums[:model_width],
            proj_sums[2 * model_width :],
            jnp.sum(d_branch.astype(jnp.float32), axis=0),
            d_gain_two,
            d_shift_two,
            jnp.sum(back_rows, axis=0),
        ],
        axis=1,
    )
    grad_s_local = jnp.concatenate(
        [small_cols, jnp.sum(d_pre.astype(jnp.float32), axis=0).reshape(model_width, -1)], axis=1
    )
    part_w, part_s = (
        lax.psum_scatter(grad_w_local, "dp", scatter_dimension=1, tiled=True),
        lax.psum_scatter(grad_s_local, "dp", scatter_dimension=1, tiled=True),
    )
    part_w, part_s = (
        lax.psum_scatter(part_w, "fsdp", scatter_dimension=0, tiled=True),
        lax.psum_scatter(part_s, "fsdp", scatter_dimension=0, tiled=True),
    )
    grad_w, grad_s = (
        lax.all_gather(part_w, "dp", axis=1, tiled=True),
        lax.all_gather(part_s, "dp", axis=1, tiled=True),
    )
    row_count = grad_w.shape[0]
    block_width = model_width // 2
    block_count = grad_w.shape[1] // block_width
    owned_slots = first_moment.shape[0]
    devices = lax.axis_size("fsdp")
    slot_ids = jnp.arange(owned_slots * devices, dtype=jnp.int32)
    matches = block_slots[None, :] == slot_ids[:, None]
    in_use = jnp.any(matches, axis=1)
    source_block = jnp.sum(
        jnp.where(matches, jnp.arange(block_count, dtype=jnp.int32)[None, :], 0), axis=1
    )
    outgoing = jnp.take(grad_w.reshape(row_count, block_count, block_width), source_block, axis=1)
    outgoing = jnp.where(in_use[None, :, None], outgoing, 0.0).reshape(
        row_count, devices, owned_slots, block_width
    )
    incoming = lax.all_to_all(outgoing, "fsdp", split_axis=1, concat_axis=0, tiled=True).reshape(
        row_count * devices, owned_slots, block_width
    )
    my_use = lax.dynamic_slice_in_dim(in_use, lax.axis_index("fsdp") * owned_slots, owned_slots)
    eigen_turned = jnp.einsum("kdi,dkc->kic", left_bases, incoming, precision=EXACT_PRECISION)
    eigen_turned = jnp.einsum("kic,kcj->kij", eigen_turned, right_bases, precision=EXACT_PRECISION)
    first_new = BETA_FIRST * first_moment + (1.0 - BETA_FIRST) * eigen_turned
    second_new = BETA_SECOND * second_moment + (1.0 - BETA_SECOND) * eigen_turned * eigen_turned
    direction = adam_direction(first_new, second_new)
    rotated_gradient = jnp.einsum("kij,klj->kil", direction, right_bases, precision=EXACT_PRECISION)
    rotated_gradient = jnp.einsum(
        "kdi,kil->dkl", left_bases, rotated_gradient, precision=EXACT_PRECISION
    )
    returned = lax.all_to_all(
        rotated_gradient.reshape(devices, row_count, owned_slots, block_width),
        "fsdp",
        split_axis=0,
        concat_axis=0,
        tiled=True,
    )
    by_slot = jnp.moveaxis(returned, 1, 0).reshape(row_count, devices * owned_slots, block_width)
    update = jnp.take(by_slot, block_slots, axis=1).reshape(row_count, block_count * block_width)
    new_master = master - RATE_MATRIX * update
    new_copy = new_master.astype(jnp.bfloat16)
    keep_slot = my_use[:, None, None]
    new_first = jnp.where(keep_slot, first_new, 0.0)
    new_second = jnp.where(keep_slot, second_new, 0.0)
    new_small_first = BETA_FIRST * small_first + (1.0 - BETA_FIRST) * grad_s
    new_small_second = BETA_SECOND * small_second + (1.0 - BETA_SECOND) * grad_s * grad_s
    new_small = small_params - RATE_VECTOR * adam_direction(new_small_first, new_small_second)
    return (
        out_tokens,
        grad_tokens,
        grad_w,
        grad_s,
        new_first,
        new_second,
        new_master,
        new_copy,
        new_small,
        new_small_first,
        new_small_second,
        loss_accuracy,
        counts,
    )


def solution(mesh):
    return jax.shard_map(
        local,
        mesh=mesh,
        in_specs=(
            P(("dp", "fsdp"), None),
            P(("dp", "fsdp"), None),
            P(("dp", "fsdp")),
            P(("dp", "fsdp")),
            P(),
            P("fsdp", None),
            P("fsdp", None),
            P("fsdp", None),
            P("fsdp", None),
            P(),
            P("fsdp", None, None),
            P("fsdp", None, None),
            P("fsdp", None, None),
            P("fsdp", None, None),
        ),
        out_specs=(
            P(("dp", "fsdp"), None),
            P(("dp", "fsdp"), None),
            P("fsdp", None),
            P("fsdp", None),
            P("fsdp", None, None),
            P("fsdp", None, None),
            P("fsdp", None),
            P("fsdp", None),
            P("fsdp", None),
            P("fsdp", None),
            P("fsdp", None),
            P(),
            P(),
        ),
        check_vma=False,
    )
```

profile of v0, /device:TPU:0, one launch (start us, length us, event | category | flops | bytes accessed | tf_op | source)
XLA Modules:
  0.0 1169.3 jit_solution(2485766205392647652)
XLA Ops:
  7.3 3.8 convert_element_type.121
  11.2 33.4 %all-gather = bf16[8,80,16]{1,2,0:T(8,128)(2,1)S(1)} all-gather(bf16[1,80,16]{1,2,0:T(8,128)(2,1)S(1)} %convert_bitcast_fusion), channel_id=1, replica_groups=mesh['dp'=4,'fsdp'=8] {'fsdp'}, dimensions={0}, use_global_device_ids=true | all-gather | bytes 23040 | tf_op jit(solution)/shard_map/all_gather | solution.py:117
  46.0 190.6 %all-gather.5.cloned.1.call-done = bf16[640,12800]{1,0:T(8,128)(2,1)} async-done(((bf16[80,12800]{1,0:T(8,128)(2,1)}), bf16[640,12800]{1,0:T(8,128)(2,1)}) %all-gather.5.cloned.1.call-update) | async-done | bytes 16384016 | tf_op jit(solution)/shard_map/all_gather | solution.py:116
  236.6 2.8 fusion.29
  239.4 0.9 fusion.87
  240.5 1.3 copy.111
  241.8 2.0 copy.110
  243.8 0.9 multiply_reduce_fusion.1
  244.7 0.9 fusion.15
  245.7 1.1 fusion.45
  247.3 1.9 slice-done.3
  249.2 1.4 slice-done.4
  250.6 1.1 slice-done.5
  252.5 15.0 %multiply_convert_fusion.1 = (bf16[256,5120]{1,0:T(8,128)(2,1)}, f32[256,5120]{1,0:T(8,128)}, f32[256,5120]{1,0:T(8,128)}) fusion(f32[5120]{0:T(1024)S(1)} %add.172, bf16[640,12800]{1,0:T(8,128)(2,1)S(1)} %bitcast.115, f32[256,640]{1,0:T(8,128)S(1)} %get-tuple-element.106, f32[640]{0:T(1024)S(1)} %get-tuple-element.67, f32[640]{0:T(1024)S(1)} %get-tuple-element.68, ...), kind=kOutput, calls=%fused_computation.21 | convolution fusion | flops 1765048320 | bytes 20346880 | tf_op jit(solution)/shard_map/dot_general | solution.py:150
  267.5 6.6 convert_reduce_fusion
  274.1 2.4 multiply_reduce_fusion.2
  276.9 0.9 copy-done.6
  278.0 1.6 fusion.92
  279.5 1.2 convolution_convert_fusion
  280.7 1.9 copy.115
  282.6 3.7 fusion.48
  286.9 1.4 multiply_reduce_fusion
  288.3 1.4 multiply_convert_fusion
  291.4 6.7 fusion.80
  298.1 6.6 convolution_bitcast_fusion
  304.7 3.3 fusion.76
  308.0 21.8 %pad_maximum_fusion = f32[640,12800]{1,0:T(8,128)} fusion(f32[640,5120]{1,0:T(8,128)} %convolution_bitcast_fusion, f32[640,5120]{1,0:T(8,128)} %fusion.80, f32[640,640]{1,0:T(8,128)S(1)} %copy-done.5, f32[640,1920]{1,0:T(8,128)} %fusion.76), kind=kLoop, calls=%fused_computation.2 | loop fusion | flops 24576000 | bytes 65536000 | tf_op jit(solution)/shard_map/concatenate | solution.py:218
  329.9 225.7 %reduce-scatter.5.cloned.1.call-done = f32[640,3200]{1,0:T(8,128)} async-done(((f32[640,12800]{1,0:T(8,128)}), f32[640,3200]{1,0:T(8,128)}) %reduce-scatter.5.cloned.1.call-update) | async-done | bytes 8192016 | tf_op jit(solution)/shard_map/reduce_scatter | solution.py:245
  555.7 149.0 %reduce-scatter.7.cloned.1.call-done = f32[80,3200]{1,0:T(8,128)} async-done(((f32[640,3200]{1,0:T(8,128)}), f32[80,3200]{1,0:T(8,128)}) %reduce-scatter.7.cloned.1.call-update) | async-done | bytes 1024016 | tf_op jit(solution)/shard_map/reduce_scatter | solution.py:249
  705.0 34.2 %all-gather.7.cloned.1.call-done = f32[80,12800]{1,0:T(8,128)} async-done(((f32[80,3200]{1,0:T(8,128)}), f32[80,12800]{1,0:T(8,128)}) %all-gather.7.cloned.1.call-update) | async-done | bytes 4096016 | tf_op jit(solution)/shard_map/all_gather | solution.py:253
  739.2 5.7 reshape.267
  744.9 5.5 copy.130
  750.4 5.5 gather_fusion
  755.9 5.6 bitcast_select_fusion
  761.6 5.5 all-to-all-start
  767.1 109.1 %all-to-all-done = f32[80,8,5,320]{3,0,2,1:T(8,128)} async-done(((f32[80,8,5,320]{3,0,2,1:T(8,128)}), f32[80,8,5,320]{3,0,2,1:T(8,128)}, u32[]{:S(2)}, u32[]{:S(2)}) %all-to-all-start) | async-done | bytes 4096032 | tf_op jit(solution)/shard_map/all_to_all | solution.py:271
  876.2 2.8 copy.131
  879.0 33.4 %fusion.93 = f32[5,320,640]{2,1,0:T(8,128)S(1)} fusion(f32[640,5,320]{2,0,1:T(8,128)S(1)} %bitcast.89, f32[5,640,640]{2,1,0:T(8,128)} %param.28), kind=kOutput, calls=%fused_computation.168 | convolution fusion | flops 7864320000 | bytes 16384000 | tf_op jit(solution)/shard_map/kdi,dkc->kic/dot_general | solution.py:275
  912.4 18.5 %broadcast_select_fusion = (f32[5,640,320]{1,2,0:T(8,128)}, f32[5,640,320]{1,2,0:T(8,128)}, f32[5,640,320]{1,2,0:T(8,128)}) fusion(pred[5]{0:T(512)(128)(4,1)S(1)} %dynamic_slice.21, f32[5,640,320]{1,2,0:T(8,128)} %param.27, f32[5,640,320]{1,2,0:T(8,128)} %param.26, f32[5,320,640]{2,1,0:T(8,128)S(1)} %fusion.93, f32[5,320,320]{2,1,0:T(8,128)S(1)} %copy-done), kind=kOutput, calls=%fused_computation.61 | convolution fusion | flops 3940352000 | bytes 26624004 | tf_op jit(solution)/shard_map/kic,kcj->kij/dot_general | solution.py:276
  930.9 19.0 %fusion.17 = f32[5,640,320]{1,2,0:T(8,128)S(1)} fusion(f32[5,320,320]{2,1,0:T(8,128)S(1)} %copy-done, f32[5,640,320]{1,2,0:T(8,128)} %get-tuple-element.114, f32[5,640,320]{1,2,0:T(8,128)} %param.26, f32[5,640,320]{1,2,0:T(8,128)} %param.27), kind=kOutput, calls=%fused_computation.42 | convolution fusion | flops 3942400000 | bytes 18432000 | tf_op jit(solution)/shard_map/kij,klj->kil/dot_general | solution.py:280
  950.0 20.1 %convolution_bitcast_fusion.1 = f32[640,5,320]{0,2,1:T(8,128)} fusion(f32[5,640,320]{1,2,0:T(8,128)S(1)} %fusion.17, f32[5,640,640]{2,1,0:T(8,128)S(1)} %bitcast.87), kind=kOutput, calls=%fused_computation.58 | convolution fusion | flops 7864320000 | bytes 16384000 | tf_op jit(solution)/shard_map/kdi,kil->dkl/dot_general | solution.py:281
  970.2 6.6 copy.134
  976.7 4.9 copy.135
  981.7 4.7 all-to-all-start.1
  988.0 0.9 reshape.266
  989.8 0.9 stack.38
  991.6 1.6 convert_reduce_fusion.1
  994.0 3.1 fusion.81
  997.6 1.1 convert_reduce_fusion.3
  998.8 0.9 stack.39
  1002.3 2.3 concatenate.21
  1004.6 15.0 %all-reduce = f32[640,16]{1,0:T(8,128)} all-reduce(f32[640,16]{1,0:T(8,128)S(1)} %concatenate.21), channel_id=4, replica_groups=mesh['dp'=4,'fsdp'=8] {'dp'}, use_global_device_ids=true, to_apply=%region_21.22.clone | all-reduce | flops 10240 | bytes 81920
  1019.6 1.8 constant_dynamic-slice_fusion
  1021.5 5.9 fusion.42
  1029.3 88.3 %all-reduce.1 = (f32[4]{0:T(128)S(1)}, f32[5]{0:T(128)S(1)}) all-reduce(f32[4]{0:T(128)S(1)} %get-tuple-element.77, f32[5]{0:T(128)S(1)} %pad_maximum_fusion.3), channel_id=1, replica_groups=mesh['dp'=4,'fsdp'=8] {'dp','fsdp'}, use_global_device_ids=true, to_apply=%region_33.35 | all-reduce | flops 9 | bytes 72 | tf_op jit(solution)/shard_map/psum | solution.py:174
  1117.6 1.1 fusion.89
  1120.0 8.9 reduce-scatter.9.cloned.1.call-done
  1129.7 5.2 all-gather.1
  1135.5 5.5 gather_fusion.1
  1141.0 3.0 bitcast_multiply_fusion
  1144.1 3.7 copy.136
  1147.8 5.5 mul.298
  1153.3 6.7 fusion.83
  1160.0 2.0 copy.148
  (153 shorter events, 17.4 us)
Async XLA Ops:
  7.2 905.2 %copy-start = (f32[5,320,320]{2,1,0:T(8,128)S(1)}, f32[5,320,320]{2,1,0:T(8,128)}, u32[]{:S(2)}) copy-start(f32[5,320,320]{2,1,0:T(8,128)} %param.29) | copy-start | bytes 6144004
  7.2 4.0 copy-start.25
  7.2 38.5 %copy-start.4 = (bf16[256,640]{1,0:T(8,128)(2,1)S(1)}, bf16[256,640]{1,0:T(8,128)(2,1)}, u32[]{:S(2)}) copy-start(bf16[256,640]{1,0:T(8,128)(2,1)} %param.16) | copy-start | bytes 983044
  7.2 229.4 %all-gather.5.cloned.1.call-start = ((), (), s32[]{:S(2)}) async-start(), calls=%async_computation.5 | async-start | bytes 18432000 | tf_op jit(solution)/shard_map/all_gather | solution.py:116
  11.1 544.6 %reduce-scatter.5.cloned.1.call-start = ((), (), s32[]{:S(2)}) async-start(), calls=%async_computation.6 | async-start | bytes 40960000 | tf_op jit(solution)/shard_map/reduce_scatter | solution.py:245
  46.0 198.6 %copy-start.27 = (f32[256]{0:T(256)}, f32[256]{0:T(256)S(1)}, u32[]{:S(2)}) copy-start(f32[256]{0:T(256)S(1)} %fusion.63) | copy-start | bytes 3076
  240.5 5.1 copy-start.12
  241.7 3.9 copy-start.14
  243.8 1.9 copy-start.22
  243.8 3.6 slice-start.2
  244.7 2.7 copy-start.1
  244.7 4.5 slice-start.3
  245.6 4.9 slice-start.4
  245.7 6.0 slice-start.5
  252.5 15.0 %copy-start.16 = (bf16[256,640]{1,0:T(8,128)(2,1)S(1)}, bf16[256,640]{1,0:T(8,128)(2,1)}, u32[]{:S(2)}) copy-start(bf16[256,640]{1,0:T(8,128)(2,1)} %param.17) | copy-start | bytes 983044
  274.1 2.4 copy-start.19
  276.9 0.9 copy-start.6
  282.6 4.1 copy-start.2
  282.6 4.2 copy-start.9
  282.6 4.3 copy-start.23
  286.9 17.8 %copy-start.8 = (bf16[20,32,256]{2,1,0:T(8,128)(2,1)}, bf16[20,32,256]{2,1,0:T(8,128)(2,1)S(1)}, u32[]{:S(2)}) copy-start(bf16[20,32,256]{2,1,0:T(8,128)(2,1)S(1)} %fusion.48) | copy-start | bytes 983044
  288.2 1.4 copy-start.15
  288.2 2.3 copy-start.13
  289.7 1.7 copy-start.20
  290.6 14.1 %copy-start.10 = (bf16[20,32,256]{2,1,0:T(8,128)(2,1)}, bf16[20,32,256]{2,1,0:T(8,128)(2,1)S(1)}, u32[]{:S(2)}) copy-start(bf16[20,32,256]{2,1,0:T(8,128)(2,1)S(1)} %fusion.47) | copy-start | bytes 983044
  291.4 13.3 %copy-start.11 = (bf16[20,32,256]{2,1,0:T(8,128)(2,1)}, bf16[20,32,256]{2,1,0:T(8,128)(2,1)S(1)}, u32[]{:S(2)}) copy-start(bf16[20,32,256]{2,1,0:T(8,128)(2,1)S(1)} %fusion.46) | copy-start | bytes 983044
  291.4 6.7 copy-start.17
  291.4 6.7 copy-start.21
  304.7 3.3 copy-start.5
  329.9 374.9 %copy-start.35 = (s32[40]{0:T(128)S(1)}, s32[40]{0:T(128)}, u32[]{:S(2)}) copy-start(s32[40]{0:T(128)} %param.25) | copy-start | bytes 484
  329.9 374.8 %reduce-scatter.7.cloned.1.call-start = ((), (), s32[]{:S(2)}) async-start(), calls=%async_computation.7 | async-start | bytes 9216000 | tf_op jit(solution)/shard_map/reduce_scatter | solution.py:249
  555.7 183.5 %all-gather.7.cloned.1.call-start = ((), (), s32[]{:S(2)}) async-start(), calls=%async_computation.8 | async-start | bytes 5120000 | tf_op jit(solution)/shard_map/all_gather | solution.py:253
  761.6 114.7 %all-to-all-start = ((f32[80,8,5,320]{3,0,2,1:T(8,128)}), f32[80,8,5,320]{3,0,2,1:T(8,128)}, u32[]{:S(2)}, u32[]{:S(2)}) async-start(f32[80,8,5,320]{3,0,2,1:T(8,128)} %bitcast.88), calls=%async_computation.3 | async-start | bytes 9830400 | tf_op jit(solution)/shard_map/all_to_all | solution.py:271
  879.0 71.0 %slice-start = ((s8[8192000]{0:T(1024)(128)(4,1)}), s8[4194304]{0:T(1024)(128)(4,1)S(1)}, s32[]{:S(2)}) async-start(s8[8192000]{0:T(1024)(128)(4,1)} %bitcast.86), calls=%async_computation.10 | async-start | bytes 8388608
  912.4 37.6 %slice-start.1 = ((s8[8192000]{0:T(1024)(128)(4,1)}), s8[3997696]{0:T(1024)(128)(4,1)S(1)}, s32[]{:S(2)}) async-start(s8[8192000]{0:T(1024)(128)(4,1)} %bitcast.86), calls=%async_computation.11 | async-start | bytes 7995392
  981.7 5.0 copy-start.32
  981.7 5.0 copy-start.36
  981.7 153.8 %all-to-all-start.1 = ((f32[8,80,5,320]{3,1,2,0:T(8,128)}), f32[8,80,5,320]{3,1,2,0:T(8,128)}, u32[]{:S(2)}, u32[]{:S(2)}) async-start(f32[8,80,5,320]{3,1,2,0:T(8,128)} %copy.135), calls=%async_computation.4 | async-start | bytes 9830400 | tf_op jit(solution)/shard_map/all_to_all | solution.py:284
  986.4 142.4 %reduce-scatter.9.cloned.1.call-start = ((), (), s32[]{:S(2)}) async-start(), calls=%async_computation.9 | async-start | bytes 368640 | tf_op jit(solution)/shard_map/reduce_scatter | solution.py:250
  988.9 8.3 copy-start.28
  991.6 6.1 copy-start.7
  991.6 6.1 copy-start.18
  997.2 24.3 %copy-start.34 = (f32[640]{0:T(1024)S(1)}, f32[640]{0:T(1024)}, u32[]{:S(2)}) copy-start(f32[640]{0:T(1024)} %get-tuple-element.66) | copy-start | bytes 7684
  1021.5 6.0 copy-start.31
  1021.5 6.3 copy-start.33
  1021.5 113.4 %copy-start.26 = (f32[80,16]{0,1:T(8,128)S(1)}, f32[80,16]{0,1:T(8,128)}, u32[]{:S(2)}) copy-start(f32[80,16]{0,1:T(8,128)} %param.22) | copy-start | bytes 15364
  1021.5 113.4 %copy-start.29 = (f32[80,16]{0,1:T(8,128)S(1)}, f32[80,16]{0,1:T(8,128)}, u32[]{:S(2)}) copy-start(f32[80,16]{0,1:T(8,128)} %param.23) | copy-start | bytes 15364
  1021.5 113.4 %copy-start.30 = (f32[80,16]{0,1:T(8,128)S(1)}, f32[80,16]{0,1:T(8,128)}, u32[]{:S(2)}) copy-start(f32[80,16]{0,1:T(8,128)} %param.24) | copy-start | bytes 15364
  1027.5 116.6 %copy-start.24 = (bf16[256,640]{1,0:T(8,128)(2,1)}, bf16[256,640]{1,0:T(8,128)(2,1)S(1)}, u32[]{:S(2)}) copy-start(bf16[256,640]{1,0:T(8,128)(2,1)S(1)} %fusion.42) | copy-start | bytes 983044
  1153.3 6.7 copy-start.3
Sparse Core Ops, SparseCore 0:
  11.2 225.3 all-gather.4
  330.0 225.6 reduce-scatter.4
  559.4 145.2 reduce-scatter.6
  706.1 32.9 all-gather.6
  1021.6 107.2 reduce-scatter.8
where the time goes:
time: 1180 us; the launch traced here: 1170 us
  waiting for transfers between devices  717 us (61%)
  matrix products  156 us (13%)
  blocking collectives  142 us (12%)
  local copies, waits for them, and re-layouts  76.1 us (6%)
  other arithmetic  51.6 us (4%)
  between operations  16 us (1%)
    reduce_scatter x1, waiting for transfers between devices, local(): lax.psum_scatter(grad_w_local, 'dp', scatter_dimension=1, tiled=True)  226 us
    all_gather x1, waiting for transfers between devices, local(): lax.all_gather(local_weights, 'fsdp', axis=0, tiled=True)  191 us
    reduce_scatter x1, waiting for transfers between devices, local(): lax.psum_scatter(part_w, 'fsdp', scatter_dimension=0, tiled=True)  149 us
    all_to_all x1, waiting for transfers between devices, local(): lax.all_to_all(outgoing, 'fsdp', split_axis=1, concat_axis=0, tiled=True)  109 us
    psum x1, blocking collectives, local(): lax.psum((local_sums, jnp.sum(chosen, axis=0)), ('dp', 'fsdp'))  88.3 us
    all_gather x1, waiting for transfers between devices, local(): lax.all_gather(part_w, 'dp', axis=1, tiled=True)  34.2 us
    all_gather x1, blocking collectives, local(): lax.all_gather(local_small, 'fsdp', axis=0, tiled=True)  33.4 us
    dot_general x1, matrix products, local(): jnp.einsum('kdi,dkc->kic', left_bases, incoming, precision=EXACT_PRECISION)  33.4 us
  transfers between devices with their start and end apart: 7, of which 6 were waited for; matrix products, arithmetic and copies ran while one was open for 3% of the time, Pallas kernels for 0%

commit v1 on v0

--- a/solution.py
+++ b/solution.py
@@ -268,9 +268,9 @@
     outgoing = jnp.where(in_use[None, :, None], outgoing, 0.0).reshape(
         row_count, devices, owned_slots, block_width
     )
-    incoming = lax.all_to_all(outgoing, "fsdp", split_axis=1, concat_axis=0, tiled=True).reshape(
-        row_count * devices, owned_slots, block_width
-    )
+    incoming = jnp.concatenate(
+        lax.all_to_all(jnp.stack(jnp.split(outgoing, lax.axis_size("fsdp"), 1)), "fsdp", 0, 0), 0
+    ).reshape(row_count * devices, owned_slots, block_width)
     my_use = lax.dynamic_slice_in_dim(in_use, lax.axis_index("fsdp") * owned_slots, owned_slots)
     eigen_turned = jnp.einsum("kdi,dkc->kic", left_bases, incoming, precision=EXACT_PRECISION)
     eigen_turned = jnp.einsum("kic,kcj->kij", eigen_turned, right_bases, precision=EXACT_PRECISION)

time: 1180 us -> 1180 us (level)
  no operation moved by 1% of the time
where the time goes in v1:
time: 1180 us; the launch traced here: 1170 us
  waiting for transfers between devices  717 us (61%)
  matrix products  156 us (13%)
  blocking collectives  142 us (12%)
  local copies, waits for them, and re-layouts  83.2 us (7%)
  other arithmetic  49.4 us (4%)
  between operations  16.1 us (1%)
    reduce_scatter x1, waiting for transfers between devices, local(): lax.psum_scatter(grad_w_local, 'dp', scatter_dimension=1, tiled=True)  226 us
    all_gather x1, waiting for transfers between devices, local(): lax.all_gather(local_weights, 'fsdp', axis=0, tiled=True)  191 us
    reduce_scatter x1, waiting for transfers between devices, local(): lax.psum_scatter(part_w, 'fsdp', scatter_dimension=0, tiled=True)  149 us
    all_to_all x1, waiting for transfers between devices, local(): lax.all_to_all(jnp.stack(jnp.split(outgoing, lax.axis_size('fsdp'), 1)),...  109 us
    psum x1, blocking collectives, local(): lax.psum((local_sums, jnp.sum(chosen, axis=0)), ('dp', 'fsdp'))  88.3 us
    all_gather x1, waiting for transfers between devices, local(): lax.all_gather(part_w, 'dp', axis=1, tiled=True)  34.2 us
    all_gather x1, blocking collectives, local(): lax.all_gather(local_small, 'fsdp', axis=0, tiled=True)  33.4 us
    dot_general x1, matrix products, local(): jnp.einsum('kdi,dkc->kic', left_bases, incoming, precision=EXACT_PRECISION)  33.4 us
  transfers between devices with their start and end apart: 7, of which 6 were waited for; matrix products, arithmetic and copies ran while one was open for 3% of the time, Pallas kernels for 0%

profile of v1, /device:TPU:0, one launch (start us, length us, event | category | flops | bytes accessed | tf_op | source)
XLA Modules:
  0.0 1174.1 jit_solution(5509462171209980996)
XLA Ops:
  7.3 3.8 convert_element_type.121
  11.2 33.4 %all-gather = bf16[8,80,16]{1,2,0:T(8,128)(2,1)S(1)} all-gather(bf16[1,80,16]{1,2,0:T(8,128)(2,1)S(1)} %convert_bitcast_fusion), channel_id=1, replica_groups=mesh['dp'=4,'fsdp'=8] {'fsdp'}, dimensions={0}, use_global_device_ids=true | all-gather | bytes 23040 | tf_op jit(solution)/shard_map/all_gather | solution.py:117
  46.0 190.6 %all-gather.5.cloned.1.call-done = bf16[640,12800]{1,0:T(8,128)(2,1)} async-done(((bf16[80,12800]{1,0:T(8,128)(2,1)}), bf16[640,12800]{1,0:T(8,128)(2,1)}) %all-gather.5.cloned.1.call-update) | async-done | bytes 16384016 | tf_op jit(solution)/shard_map/all_gather | solution.py:116
  236.6 2.8 fusion.29
  239.4 0.9 fusion.95
  240.5 1.3 copy.117
  241.8 2.0 copy.116
  243.8 0.9 multiply_reduce_fusion.1
  244.7 0.9 fusion.15
  245.7 1.1 fusion.45
  247.3 1.9 slice-done.3
  249.2 1.4 slice-done.4
  250.6 1.1 slice-done.5
  252.5 15.0 %multiply_convert_fusion.1 = (bf16[256,5120]{1,0:T(8,128)(2,1)}, f32[256,5120]{1,0:T(8,128)}, f32[256,5120]{1,0:T(8,128)}) fusion(f32[5120]{0:T(1024)S(1)} %add.172, bf16[640,12800]{1,0:T(8,128)(2,1)S(1)} %bitcast.151, f32[256,640]{1,0:T(8,128)S(1)} %get-tuple-element.106, f32[640]{0:T(1024)S(1)} %get-tuple-element.67, f32[640]{0:T(1024)S(1)} %get-tuple-element.68, ...), kind=kOutput, calls=%fused_computation.21 | convolution fusion | flops 1765048320 | bytes 20346880 | tf_op jit(solution)/shard_map/dot_general | solution.py:150
  267.5 6.6 convert_reduce_fusion
  274.1 2.4 multiply_reduce_fusion.2
  278.0 1.6 fusion.100
  279.5 1.2 convolution_convert_fusion
  280.7 1.9 copy.121
  282.6 3.7 fusion.48
  286.9 1.4 multiply_reduce_fusion
  288.3 1.4 multiply_convert_fusion
  291.4 6.7 fusion.88
  298.1 6.6 convolution_bitcast_fusion
  304.7 3.3 fusion.84
  308.0 21.8 %pad_maximum_fusion = f32[640,12800]{1,0:T(8,128)} fusion(f32[640,5120]{1,0:T(8,128)} %convolution_bitcast_fusion, f32[640,5120]{1,0:T(8,128)} %fusion.88, f32[640,640]{1,0:T(8,128)S(1)} %copy-done.5, f32[640,1920]{1,0:T(8,128)} %fusion.84), kind=kLoop, calls=%fused_computation.2 | loop fusion | flops 24576000 | bytes 65536000 | tf_op jit(solution)/shard_map/concatenate | solution.py:218
  329.9 225.7 %reduce-scatter.5.cloned.1.call-done = f32[640,3200]{1,0:T(8,128)} async-done(((f32[640,12800]{1,0:T(8,128)}), f32[640,3200]{1,0:T(8,128)}) %reduce-scatter.5.cloned.1.call-update) | async-done | bytes 8192016 | tf_op jit(solution)/shard_map/reduce_scatter | solution.py:245
  555.7 149.0 %reduce-scatter.7.cloned.1.call-done = f32[80,3200]{1,0:T(8,128)} async-done(((f32[640,3200]{1,0:T(8,128)}), f32[80,3200]{1,0:T(8,128)}) %reduce-scatter.7.cloned.1.call-update) | async-done | bytes 1024016 | tf_op jit(solution)/shard_map/reduce_scatter | solution.py:249
  705.0 34.2 %all-gather.7.cloned.1.call-done = f32[80,12800]{1,0:T(8,128)} async-done(((f32[80,3200]{1,0:T(8,128)}), f32[80,12800]{1,0:T(8,128)}) %all-gather.7.cloned.1.call-update) | async-done | bytes 4096016 | tf_op jit(solution)/shard_map/all_gather | solution.py:253
  739.2 5.7 reshape.263
  744.9 5.5 copy.136
  750.4 5.5 gather_fusion
  755.9 3.4 bitcast_select_fusion
  763.7 0.9 fusion.67
  764.6 0.9 fusion.66
  766.4 5.5 all-to-all-start
  772.0 109.1 %all-to-all-done = f32[8,80,1,5,320]{4,1,3,2,0:T(8,128)} async-done(((f32[8,80,1,5,320]{4,1,3,2,0:T(8,128)}), f32[8,80,1,5,320]{4,1,3,2,0:T(8,128)}, u32[]{:S(2)}, u32[]{:S(2)}) %all-to-all-start) | async-done | bytes 4096032 | tf_op jit(solution)/shard_map/all_to_all | solution.py:272
  881.1 2.8 copy.137
  883.9 33.4 %fusion.101 = f32[5,320,640]{2,1,0:T(8,128)S(1)} fusion(f32[640,5,320]{2,0,1:T(8,128)S(1)} %bitcast.125, f32[5,640,640]{2,1,0:T(8,128)} %param.28), kind=kOutput, calls=%fused_computation.184 | convolution fusion | flops 7864320000 | bytes 16384000 | tf_op jit(solution)/shard_map/kdi,dkc->kic/dot_general | solution.py:275
  917.3 18.5 %broadcast_select_fusion = (f32[5,640,320]{1,2,0:T(8,128)}, f32[5,640,320]{1,2,0:T(8,128)}, f32[5,640,320]{1,2,0:T(8,128)}) fusion(pred[5]{0:T(512)(128)(4,1)S(1)} %dynamic_slice.21, f32[5,640,320]{1,2,0:T(8,128)} %param.27, f32[5,640,320]{1,2,0:T(8,128)} %param.26, f32[5,320,640]{2,1,0:T(8,128)S(1)} %fusion.101, f32[5,320,320]{2,1,0:T(8,128)S(1)} %copy-done), kind=kOutput, calls=%fused_computation.61 | convolution fusion | flops 3940352000 | bytes 26624004 | tf_op jit(solution)/shard_map/kic,kcj->kij/dot_general | solution.py:276
  935.8 19.0 %fusion.17 = f32[5,640,320]{1,2,0:T(8,128)S(1)} fusion(f32[5,320,320]{2,1,0:T(8,128)S(1)} %copy-done, f32[5,640,320]{1,2,0:T(8,128)} %get-tuple-element.114, f32[5,640,320]{1,2,0:T(8,128)} %param.26, f32[5,640,320]{1,2,0:T(8,128)} %param.27), kind=kOutput, calls=%fused_computation.42 | convolution fusion | flops 3942400000 | bytes 18432000 | tf_op jit(solution)/shard_map/kij,klj->kil/dot_general | solution.py:280
  954.9 20.1 %convolution_bitcast_fusion.1 = f32[640,5,320]{0,2,1:T(8,128)} fusion(f32[5,640,320]{1,2,0:T(8,128)S(1)} %fusion.17, f32[5,640,640]{2,1,0:T(8,128)S(1)} %bitcast.116), kind=kOutput, calls=%fused_computation.58 | convolution fusion | flops 7864320000 | bytes 16384000 | tf_op jit(solution)/shard_map/kdi,kil->dkl/dot_general | solution.py:281
  975.0 6.6 copy.140
  981.6 4.9 copy.141
  986.5 4.7 all-to-all-start.1
  992.8 0.9 reshape.262
  994.6 0.9 stack.74
  996.4 1.6 convert_reduce_fusion.1
  998.9 3.1 fusion.89
  1002.5 1.1 convert_reduce_fusion.3
  1007.1 2.3 concatenate.21
  1009.4 15.0 %all-reduce = f32[640,16]{1,0:T(8,128)} all-reduce(f32[640,16]{1,0:T(8,128)S(1)} %concatenate.21), channel_id=4, replica_groups=mesh['dp'=4,'fsdp'=8] {'dp'}, use_global_device_ids=true, to_apply=%region_21.22.clone | all-reduce | flops 10240 | bytes 81920
  1024.4 1.8 constant_dynamic-slice_fusion
  1026.4 5.9 fusion.42
  1034.1 88.3 %all-reduce.1 = (f32[4]{0:T(128)S(1)}, f32[5]{0:T(128)S(1)}) all-reduce(f32[4]{0:T(128)S(1)} %get-tuple-element.77, f32[5]{0:T(128)S(1)} %pad_maximum_fusion.3), channel_id=1, replica_groups=mesh['dp'=4,'fsdp'=8] {'dp','fsdp'}, use_global_device_ids=true, to_apply=%region_33.35 | all-reduce | flops 9 | bytes 72 | tf_op jit(solution)/shard_map/psum | solution.py:174
  1122.5 1.1 fusion.97
  1124.8 8.8 reduce-scatter.9.cloned.1.call-done
  1134.5 5.2 all-gather.1
  1140.3 5.5 gather_fusion.1
  1145.8 3.0 bitcast_multiply_fusion
  1148.9 3.7 copy.142
  1152.6 5.5 mul.298
  1158.1 6.7 fusion.91
  1164.8 2.0 copy.161
  (161 shorter events, 24.4 us)
Async XLA Ops:
  7.2 910.1 %copy-start = (f32[5,320,320]{2,1,0:T(8,128)S(1)}, f32[5,320,320]{2,1,0:T(8,128)}, u32[]{:S(2)}) copy-start(f32[5,320,320]{2,1,0:T(8,128)} %param.29) | copy-start | bytes 6144004
  7.2 4.0 copy-start.25
  7.2 38.5 %copy-start.4 = (bf16[256,640]{1,0:T(8,128)(2,1)S(1)}, bf16[256,640]{1,0:T(8,128)(2,1)}, u32[]{:S(2)}) copy-start(bf16[256,640]{1,0:T(8,128)(2,1)} %param.16) | copy-start | bytes 983044
  7.2 229.4 %all-gather.5.cloned.1.call-start = ((), (), s32[]{:S(2)}) async-start(), calls=%async_computation.5 | async-start | bytes 18432000 | tf_op jit(solution)/shard_map/all_gather | solution.py:116
  11.1 544.6 %reduce-scatter.5.cloned.1.call-start = ((), (), s32[]{:S(2)}) async-start(), calls=%async_computation.6 | async-start | bytes 40960000 | tf_op jit(solution)/shard_map/reduce_scatter | solution.py:245
  46.0 198.6 %copy-start.27 = (f32[256]{0:T(256)}, f32[256]{0:T(256)S(1)}, u32[]{:S(2)}) copy-start(f32[256]{0:T(256)S(1)} %fusion.63) | copy-start | bytes 3076
  240.5 5.1 copy-start.12
  241.7 3.9 copy-start.14
  243.8 1.9 copy-start.22
  243.8 3.6 slice-start.2
  244.7 2.7 copy-start.1
  244.7 4.5 slice-start.3
  245.6 4.9 slice-start.4
  245.7 6.0 slice-start.5
  252.5 15.0 %copy-start.16 = (bf16[256,640]{1,0:T(8,128)(2,1)S(1)}, bf16[256,640]{1,0:T(8,128)(2,1)}, u32[]{:S(2)}) copy-start(bf16[256,640]{1,0:T(8,128)(2,1)} %param.17) | copy-start | bytes 983044
  274.1 2.4 copy-start.19
  276.9 0.9 copy-start.6
  282.6 4.1 copy-start.2
  282.6 4.2 copy-start.9
  282.6 4.3 copy-start.23
  286.9 17.8 %copy-start.8 = (bf16[20,32,256]{2,1,0:T(8,128)(2,1)}, bf16[20,32,256]{2,1,0:T(8,128)(2,1)S(1)}, u32[]{:S(2)}) copy-start(bf16[20,32,256]{2,1,0:T(8,128)(2,1)S(1)} %fusion.48) | copy-start | bytes 983044
  288.2 1.4 copy-start.15
  288.2 2.3 copy-start.13
  289.7 1.7 copy-start.20
  290.6 14.1 %copy-start.10 = (bf16[20,32,256]{2,1,0:T(8,128)(2,1)}, bf16[20,32,256]{2,1,0:T(8,128)(2,1)S(1)}, u32[]{:S(2)}) copy-start(bf16[20,32,256]{2,1,0:T(8,128)(2,1)S(1)} %fusion.47) | copy-start | bytes 983044
  291.4 13.3 %copy-start.11 = (bf16[20,32,256]{2,1,0:T(8,128)(2,1)}, bf16[20,32,256]{2,1,0:T(8,128)(2,1)S(1)}, u32[]{:S(2)}) copy-start(bf16[20,32,256]{2,1,0:T(8,128)(2,1)S(1)} %fusion.46) | copy-start | bytes 983044
  291.4 6.7 copy-start.17
  291.4 6.7 copy-start.21
  304.7 3.3 copy-start.5
  329.9 374.9 %copy-start.35 = (s32[40]{0:T(128)S(1)}, s32[40]{0:T(128)}, u32[]{:S(2)}) copy-start(s32[40]{0:T(128)} %param.25) | copy-start | bytes 484
  329.9 374.8 %reduce-scatter.7.cloned.1.call-start = ((), (), s32[]{:S(2)}) async-start(), calls=%async_computation.7 | async-start | bytes 9216000 | tf_op jit(solution)/shard_map/reduce_scatter | solution.py:249
  555.7 183.5 %all-gather.7.cloned.1.call-start = ((), (), s32[]{:S(2)}) async-start(), calls=%async_computation.8 | async-start | bytes 5120000 | tf_op jit(solution)/shard_map/all_gather | solution.py:253
  766.4 114.7 %all-to-all-start = ((f32[8,80,1,5,320]{4,1,3,2,0:T(8,128)}), f32[8,80,1,5,320]{4,1,3,2,0:T(8,128)}, u32[]{:S(2)}, u32[]{:S(2)}) async-start(f32[8,80,1,5,320]{4,1,3,2,0:T(8,128)} %fusion.65), calls=%async_computation.3 | async-start | bytes 9830400 | tf_op jit(solution)/shard_map/all_to_all | solution.py:272
  883.9 71.0 %slice-start = ((s8[8192000]{0:T(1024)(128)(4,1)}), s8[4194304]{0:T(1024)(128)(4,1)S(1)}, s32[]{:S(2)}) async-start(s8[8192000]{0:T(1024)(128)(4,1)} %bitcast.115), calls=%async_computation.10 | async-start | bytes 8388608
  917.2 37.6 %slice-start.1 = ((s8[8192000]{0:T(1024)(128)(4,1)}), s8[3997696]{0:T(1024)(128)(4,1)S(1)}, s32[]{:S(2)}) async-start(s8[8192000]{0:T(1024)(128)(4,1)} %bitcast.115), calls=%async_computation.11 | async-start | bytes 7995392
  986.5 5.0 copy-start.32
  986.5 5.0 copy-start.36
  986.5 153.8 %all-to-all-start.1 = ((f32[8,80,5,320]{3,1,2,0:T(8,128)}), f32[8,80,5,320]{3,1,2,0:T(8,128)}, u32[]{:S(2)}, u32[]{:S(2)}) async-start(f32[8,80,5,320]{3,1,2,0:T(8,128)} %copy.141), calls=%async_computation.4 | async-start | bytes 9830400 | tf_op jit(solution)/shard_map/all_to_all | solution.py:284
  991.3 142.4 %reduce-scatter.9.cloned.1.call-start = ((), (), s32[]{:S(2)}) async-start(), calls=%async_computation.9 | async-start | bytes 368640 | tf_op jit(solution)/shard_map/reduce_scatter | solution.py:250
  993.8 8.3 copy-start.28
  996.4 6.1 copy-start.7
  996.4 6.1 copy-start.18
  1002.0 24.3 %copy-start.34 = (f32[640]{0:T(1024)S(1)}, f32[640]{0:T(1024)}, u32[]{:S(2)}) copy-start(f32[640]{0:T(1024)} %get-tuple-element.66) | copy-start | bytes 7684
  1026.3 6.0 copy-start.31
  1026.3 6.3 copy-start.33
  1026.4 113.3 %copy-start.26 = (f32[80,16]{0,1:T(8,128)S(1)}, f32[80,16]{0,1:T(8,128)}, u32[]{:S(2)}) copy-start(f32[80,16]{0,1:T(8,128)} %param.22) | copy-start | bytes 15364
  1026.4 113.3 %copy-start.29 = (f32[80,16]{0,1:T(8,128)S(1)}, f32[80,16]{0,1:T(8,128)}, u32[]{:S(2)}) copy-start(f32[80,16]{0,1:T(8,128)} %param.23) | copy-start | bytes 15364
  1026.4 113.3 %copy-start.30 = (f32[80,16]{0,1:T(8,128)S(1)}, f32[80,16]{0,1:T(8,128)}, u32[]{:S(2)}) copy-start(f32[80,16]{0,1:T(8,128)} %param.24) | copy-start | bytes 15364
  1032.3 116.6 %copy-start.24 = (bf16[256,640]{1,0:T(8,128)(2,1)}, bf16[256,640]{1,0:T(8,128)(2,1)S(1)}, u32[]{:S(2)}) copy-start(bf16[256,640]{1,0:T(8,128)(2,1)S(1)} %fusion.42) | copy-start | bytes 983044
  1158.1 6.7 copy-start.3
Sparse Core Ops, SparseCore 0:
  11.2 225.3 all-gather.4
  330.0 225.6 reduce-scatter.4
  559.4 145.2 reduce-scatter.6
  706.1 32.9 all-gather.6
  1026.4 107.1 reduce-scatter.8
